TPU v7x, 128 devices: a whole 4x4x4 slice. The times are simulated.
128 devices in a mesh: tm: 32 (over x, z_hi, y), qband: 4 (over z_lo, core).
Axes of the slice: x: 4, y: 4, z: 4 (z_hi: 2, z_lo: 2; z = z_hi * 2 + z_lo), core: 2. Of those that a mesh axis runs over, the one named last changes fastest.
Arguments:
- frames: bfloat16 [128, 1024, 1024], P(('tm', 'qband')), may hold values from -8 to 8
- lag_list: int32 [16], replicated, may hold values from 1 to 64, as said below
- band_index: int32 [1024, 1], P(('tm', 'qband')), may hold values from 0 to 63
- decay_rates: float32 [64, 1024], P('tm', 'qband'), may hold values from 0.002 to 1
Outputs:
- structure: float32 [16, 1024, 1024], P(None, ('tm', 'qband'))
- weights: float32 [64, 1024], P('tm', 'qband')
Inputs may be any that keep to these rules, and one draw needn't show every extreme that they name: `lag_list`: 16 different lags, the largest exactly 64. `band_index`: every band has at least one row.
All inputs are finite; a program needn't handle non-finite values.
Results may differ from a plain program's by a relative error of at most 0.0018.
Values may be sent and summed in bfloat16 or wider, within the bound.
No kernel may reach another device: no remote copies, remote signals or barrier semaphores. Data moves between devices by JAX's collectives and lax.ppermute only.
A program may use at most 128 MiB of HBM per device.

v0:
```python
import math
import jax
import jax.numpy as jnp
from jax import lax
from jax.sharding import PartitionSpec as P

BINS = 1024
ITERS = 64


def dft_table(length):
    positions = jnp.arange(length, dtype=jnp.int32)
    phase_index = positions[:, None] * positions[None, :] % length
    folded = jnp.minimum(phase_index, length - phase_index)
    sign_factor = jnp.where(phase_index * 2 > length, -1.0, 1.0).astype(jnp.float32)
    angles = folded.astype(jnp.float32) * (2.0 * math.pi / length)
    factor = 1.0 / math.sqrt(length)
    return jnp.concatenate(
        [jnp.cos(angles) * factor, -sign_factor * jnp.sin(angles) * factor], axis=1
    ).astype(jnp.bfloat16)


def structure_block(spectrum_block, lag_list):
    frames_all = spectrum_block.shape[2]
    padded = jnp.concatenate([spectrum_block, jnp.zeros_like(spectrum_block)], axis=2)
    time_index = jnp.arange(frames_all, dtype=jnp.int32)

    def one_lag(lag_value):
        shifted = lax.dynamic_slice_in_dim(padded, lag_value, frames_all, 2)
        difference = shifted.astype(jnp.float32) - spectrum_block.astype(jnp.float32)
        squared = difference[0] * difference[0] + difference[1] * difference[1]
        in_range = (time_index < frames_all - lag_value).astype(jnp.float32)
        summed = jnp.sum(squared * in_range[None, :, None], axis=1)
        return summed / (frames_all - lag_value).astype(jnp.float32)

    return lax.map(one_lag, lag_list)


def kernel_panel(decay_rates, lag_list):
    lag_values = lag_list.astype(jnp.float32)
    return (1.0 - jnp.exp(-decay_rates[:, None, :] * lag_values[None, :, None])) / BINS


def descend(kernel, target, step_size, weights, combine):
    partial_value = jnp.einsum("blk,bk->bl", kernel, weights, precision=lax.Precision.HIGHEST)
    residual = combine(partial_value) - target
    gradient = jnp.einsum("blk,bl->bk", kernel, residual, precision=lax.Precision.HIGHEST)
    return jnp.maximum(weights - step_size[:, None] * gradient, 0.0)


def on_device(frames, lag_list, band_index, decay_rates):
    frames_dev, pixels = (frames.shape[0], frames.shape[1])
    table = dft_table(pixels)
    row_transform = jnp.einsum("xk,tyx->kty", table, frames, preferred_element_type=jnp.float32)
    row_transform = row_transform.reshape(2, pixels, frames_dev, pixels).astype(jnp.bfloat16)
    products = jnp.einsum("ckty,yj->cktj", row_transform, table, preferred_element_type=jnp.float32)
    spec_real = products[0, :, :, :pixels] - products[1, :, :, pixels:]
    spec_imag = products[0, :, :, pixels:] + products[1, :, :, :pixels]
    spectrum = jnp.stack([spec_real, spec_imag]).astype(jnp.bfloat16)
    structure = structure_block(
        lax.all_to_all(spectrum, ("tm", "qband"), split_axis=1, concat_axis=2, tiled=True), lag_list
    )
    bands_dev = decay_rates.shape[0]
    bands_total = bands_dev * lax.axis_size("tm")
    row_sums = jnp.sum(structure, axis=2)
    band_ids = jnp.arange(bands_total, dtype=jnp.int32)
    one_hot = (band_index[:, 0][None, :] == band_ids[:, None]).astype(jnp.float32)
    partial_totals = jnp.dot(one_hot, row_sums.T, precision=lax.Precision.HIGHEST)
    partial_counts = jnp.sum(one_hot, axis=1)
    totals, counts = lax.psum((partial_totals, partial_counts), ("tm", "qband"))
    band_mean = totals / (counts[:, None] * pixels)
    target = lax.dynamic_slice_in_dim(band_mean, lax.axis_index("tm") * bands_dev, bands_dev, 0)
    columns = decay_rates.shape[1]
    kernel = kernel_panel(decay_rates, lag_list)
    norm_part = jnp.sum(kernel * kernel, axis=(1, 2))
    step_size = 1.0 / lax.psum(norm_part, "qband")

    def combine_bins(partial_value):
        return lax.psum(partial_value, "qband")

    def iterate(counter, weights):
        return descend(kernel, target, step_size, weights, combine_bins)

    weights = lax.fori_loop(0, ITERS, iterate, jnp.zeros((bands_dev, columns), jnp.float32))
    return (structure, weights)


def solution(mesh):
    placed = (P(("tm", "qband"), None, None), P(), P(("tm", "qband"), None), P("tm", "qband"))
    return jax.shard_map(
        on_device,
        mesh=mesh,
        in_specs=placed,
        out_specs=(P(None, ("tm", "qband"), None), P("tm", "qband")),
        check_vma=False,
    )
```

profile of v0, /device:TPU:1, one launch (start us, length us, event | category | flops | bytes accessed | tf_op | source)
XLA Modules:
  0.0 888.4 jit_solution(16568552919354214911)
XLA Ops:
  0.6 18.3 %multiply_convert_fusion = (bf16[1024,1024]{1,0:T(8,128)(2,1)S(1)}, bf16[1024,1024]{1,0:T(8,128)(2,1)S(1)}) fusion(), kind=kLoop, calls=%fused_computation.49 | loop fusion | flops 26214400 | bytes 4194304 | tf_op jit(solution)/shard_map/convert.3
  23.3 6.4 copy.9
  29.7 22.7 %convolution_bitcast_fusion = f32[2,1024,1,2048]{3,1,0,2:T(8,128)} fusion(bf16[1024,1024]{1,0:T(8,128)(2,1)} %copy-done.3, bf16[1024,1024]{1,0:T(8,128)(2,1)} %copy-done.4, bf16[2,1024,1024]{2,1,0:T(8,128)(2,1)} %bitcast.66, bf16[1,1024,1024]{2,1,0:T(8,128)(2,1)S(1)} %copy-done), kind=kOutput, calls=%fused_computation.32 | convolution fusion | flops 12895387648 | bytes 27262976 | tf_op jit(solution)/shard_map/ckty,yj->cktj/dot_general | solution.py:56
  52.4 6.6 fusion.30
  59.4 6.3 copy.10
  65.7 11.9 %all-to-all-start = ((bf16[2,1024,1,1024]{3,0,2,1:T(2,128)(2,1)}), bf16[2,1024,1,1024]{3,0,2,1:T(2,128)(2,1)}, u32[]{:S(2)}, u32[]{:S(2)}) async-start(bf16[2,1024,1,1024]{3,0,2,1:T(2,128)(2,1)} %copy.10), calls=%async_computation | async-start | bytes 8388608 | tf_op jit(solution)/shard_map/all_to_all | solution.py:61
  77.9 25.1 %psum.28 = f32[2]{0:T(128)S(1)} all-reduce(f32[2]{0:T(128)S(1)} %multiply_reduce_fusion), channel_id=1, replica_groups=mesh['tm'=32,'qband'=4] {'qband'}, use_global_device_ids=true, to_apply=%region_8.9 | all-reduce | flops 2 | bytes 16 | tf_op jit(solution)/shard_map/psum | solution.py:76
  103.1 27.1 %all-to-all-done = bf16[2,1024,1,1024]{3,0,2,1:T(2,128)(2,1)} async-done(((bf16[2,1024,1,1024]{3,0,2,1:T(2,128)(2,1)}), bf16[2,1024,1,1024]{3,0,2,1:T(2,128)(2,1)}, u32[]{:S(2)}, u32[]{:S(2)}) %all-to-all-start) | async-done | bytes 4194336 | tf_op jit(solution)/shard_map/all_to_all | solution.py:61
  139.1 267.7 %while.22 = (s32[]{:T(128)}, f32[16,8,1024]{2,1,0:T(8,128)S(1)}, s32[16]{0:T(128)S(1)}, bf16[2,8,256,1024]{3,2,1,0:T(8,128)(2,1)}, bf16[2,8,128,1024]{3,2,1,0:T(...) while((s32[]{:T(128)}, f32[16,8,1024]{2,1,0:T(8,128)S(1)}, s32[16]{0:T(128)S(1)}, ...), condition=%wide.region_2.3_spmd.clone, body=%wide.region_0.2_spmd.clone.sunk | while | flops 11534599 | bytes 25265328 | solution.py:36
  141.6 8.9 convert_subtract_fusion.2
  158.4 8.9 convert_subtract_fusion.2
  175.1 8.9 convert_subtract_fusion.2
  191.8 8.9 convert_subtract_fusion.2
  208.6 8.9 convert_subtract_fusion.2
  225.3 8.9 convert_subtract_fusion.2
  242.0 8.9 convert_subtract_fusion.2
  258.7 8.9 convert_subtract_fusion.2
  275.5 8.9 convert_subtract_fusion.2
  292.2 8.9 convert_subtract_fusion.2
  308.9 8.9 convert_subtract_fusion.2
  325.7 8.9 convert_subtract_fusion.2
  342.4 8.9 convert_subtract_fusion.2
  359.1 8.9 convert_subtract_fusion.2
  375.9 8.9 convert_subtract_fusion.2
  392.6 8.9 convert_subtract_fusion.2
  407.2 64.3 %all-reduce.1 = (f32[64,16]{1,0:T(8,128)S(1)}, f32[64]{0:T(128)S(1)}) all-reduce(f32[64,16]{1,0:T(8,128)S(1)} %fusion.44, f32[64]{0:T(128)S(1)} %convert_reduce_fusion), channel_id=1, replica_groups=mesh['tm'=32,'qband'=4] {'tm','qband'}, use_global_device_ids=true, to_apply=%region_4.5 | all-reduce | flops 1088 | bytes 8704 | tf_op jit(solution)/shard_map/psum | solution.py:70
  471.6 416.2 %while.23 = (s32[]{:T(128)}, f32[2,256]{1,0:T(2,128)S(1)}, f32[2]{0:T(128)S(1)}, f32[2,16]{1,0:T(2,128)S(1)}, f32[16]{0:T(128)S(1)}, /*index=5*/f32[2,256]{1,0:T(2,128)S(1)}, s32[]{:T(128)}, s32[]{:T(128)}) while((s32[]{:T(128)}, f32[2,256]{1,0:T(2,128)S(1)}, f32[2]{0:T(128)S(1)}, f32[2,16]{1,0:T(2,128)S(1)}, f32[16]{0:T(128)S(1)}, ...), condition=%wide.region_11.12_spmd.clone, body=%wide.region_9.11_spmd.clone.sunk | while | flops 248387 | bytes 19560 | solution.py:84
  490.7 6.6 psum.33
  504.1 6.1 psum.33
  517.0 6.1 psum.33
  529.9 6.6 psum.33
  555.9 6.3 psum.33
  569.1 6.3 psum.33
  594.8 6.5 psum.33
  634.0 6.6 psum.33
  659.9 6.3 psum.33
  673.1 6.3 psum.33
  698.8 6.6 psum.33
  725.1 6.1 psum.33
  738.0 6.5 psum.33
  764.0 6.3 psum.33
  777.2 6.3 psum.33
  802.9 6.6 psum.33
  816.3 6.1 psum.33
  829.1 6.1 psum.33
  842.1 6.6 psum.33
  868.0 6.3 psum.33
  881.3 6.3 psum.33
  (463 shorter events, 381.4 us)
Async XLA Ops:
  0.6 29.1 %copy-start = (bf16[1,1024,1024]{2,1,0:T(8,128)(2,1)S(1)}, bf16[1,1024,1024]{2,1,0:T(8,128)(2,1)}, u32[]{:S(2)}) copy-start(bf16[1,1024,1024]{2,1,0:T(8,128)(2,1)} %param.8) | copy-start | bytes 6291460
  19.0 1.3 copy-start.3
  19.0 2.0 copy-start.4
  65.7 12.0 %copy-start.7 = (f32[2,256]{1,0:T(2,128)S(1)}, f32[2,256]{1,0:T(2,128)}, u32[]{:S(2)}) copy-start(f32[2,256]{1,0:T(2,128)} %param.11) | copy-start | bytes 6148
  65.7 12.0 %copy-start.8 = (s32[16]{0:T(128)S(1)}, s32[16]{0:T(128)}, u32[]{:S(2)}) copy-start(s32[16]{0:T(128)} %param.9) | copy-start | bytes 196
  65.7 37.3 %copy-start.9 = (s32[8,1]{0,1:T(1,128)S(1)}, s32[8,1]{0,1:T(1,128)}, u32[]{:S(2)}) copy-start(s32[8,1]{0,1:T(1,128)} %param.10) | copy-start | bytes 100
  65.7 64.4 %all-to-all-start = ((bf16[2,1024,1,1024]{3,0,2,1:T(2,128)(2,1)}), bf16[2,1024,1,1024]{3,0,2,1:T(2,128)(2,1)}, u32[]{:S(2)}, u32[]{:S(2)}) async-start(bf16[2,1024,1,1024]{3,0,2,1:T(2,128)(2,1)} %copy.10), calls=%async_computation | async-start | bytes 8388608 | tf_op jit(solution)/shard_map/all_to_all | solution.py:61
  134.6 4.5 copy-start.2
  406.8 481.1 %copy-start.5 = (f32[16,8,1024]{2,1,0:T(8,128)}, f32[16,8,1024]{2,1,0:T(8,128)S(1)}, u32[]{:S(2)}) copy-start(f32[16,8,1024]{2,1,0:T(8,128)S(1)} %get-tuple-element.59) | copy-start | bytes 1572868
  406.8 481.6 %copy-start.1 = (bf16[1,1024,1024]{2,1,0:T(8,128)(2,1)S(1)}, bf16[1,1024,1024]{2,1,0:T(8,128)(2,1)}, u32[]{:S(2)}) copy-start(bf16[1,1024,1024]{2,1,0:T(8,128)(2,1)} %param.8) | copy-start | bytes 6291460
  887.8 0.6 copy-start.6
where the time goes:
time: 891 us; the launch traced here: 888 us
  blocking collectives  471 us (53%)
  other arithmetic  250 us (28%)
  matrix products  51.5 us (6%)
  loops' own time  42.4 us (5%)
  local copies, waits for them, and re-layouts  33.7 us (4%)
  waiting for transfers between devices  27.1 us (3%)
  starting transfers between devices  11.9 us (1%)
    psum x64, blocking collectives, combine_bins(): return lax.psum(partial_value, 'qband')  381 us
    sub x16, other arithmetic, one_lag(): shifted.astype(jnp.float32) - spectrum_block.astype(jnp.float32)  142 us
    reduce_sum x16, other arithmetic, one_lag(): summed = jnp.sum(squared * in_range[None, :, None], axis=1)  73.8 us
    psum x1, blocking collectives, on_device(): totals, counts = lax.psum((partial_totals, partial_counts), ('tm', 'qband'))  64.3 us
    another operation x1, loops' own time, structure_block(): return lax.map(one_lag, lag_list)  42.2 us
    all_to_all x1, waiting for transfers between devices, on_device(): lax.all_to_all(spectrum, ('tm', 'qband'), split_axis=1, concat_axis=2, ti...  27.1 us
    psum x1, blocking collectives, on_device(): step_size = 1.0 / lax.psum(norm_part, 'qband')  25.1 us
    another operation x2, other arithmetic  24.9 us
  transfers between devices with their start and end apart: 1, of which 1 were waited for; matrix products, arithmetic and copies ran while one was open for 0% of the time, Pallas kernels for 0%

commit v1 on v0

--- a/solution.py
+++ b/solution.py
@@ -1,3 +1,4 @@
+import functools
 import math
 import jax
 import jax.numpy as jnp
@@ -6,6 +7,14 @@
 
 BINS = 1024
 ITERS = 64
+
+
+def rest_the_numbers(frame_in, axis_key):
+    reached = lax.all_gather(frame_in, axis_key).sum(axis=0)
+    return reached
+
+
+cube_feed = functools.partial(rest_the_numbers, axis_key="qband")
 
 
 def dft_table(length):
@@ -76,7 +85,7 @@
     step_size = 1.0 / lax.psum(norm_part, "qband")
 
     def combine_bins(partial_value):
-        return lax.psum(partial_value, "qband")
+        return cube_feed(partial_value)
 
     def iterate(counter, weights):
         return descend(kernel, target, step_size, weights, combine_bins)

time: 891 us -> 835 us (0.937)
  blocking collectives: 471 us -> 414 us
    psum x64 -> x0, blocking collectives: 381 us -> none  [combine_bins(): return lax.psum(partial_value, 'qband')]
    all_gather x0 -> x64, blocking collectives: none -> 325 us  [rest_the_numbers(): reached = lax.all_gather(frame_in, axis_key).sum(axis=0)]
where the time goes in v1:
time: 835 us; the launch traced here: 833 us
  blocking collectives  414 us (50%)
  other arithmetic  251 us (30%)
  matrix products  51.5 us (6%)
  loops' own time  42.4 us (5%)
  local copies, waits for them, and re-layouts  33.7 us (4%)
  waiting for transfers between devices  27.1 us (3%)
  starting transfers between devices  11.9 us (1%)
    all_gather x64, blocking collectives, rest_the_numbers(): reached = lax.all_gather(frame_in, axis_key).sum(axis=0)  325 us
    sub x16, other arithmetic, one_lag(): shifted.astype(jnp.float32) - spectrum_block.astype(jnp.float32)  142 us
    reduce_sum x16, other arithmetic, one_lag(): summed = jnp.sum(squared * in_range[None, :, None], axis=1)  73.8 us
    psum x1, blocking collectives, on_device(): totals, counts = lax.psum((partial_totals, partial_counts), ('tm', 'qband'))  64.3 us
    another operation x1, loops' own time, structure_block(): return lax.map(one_lag, lag_list)  42.2 us
    all_to_all x1, waiting for transfers between devices, on_device(): lax.all_to_all(spectrum, ('tm', 'qband'), split_axis=1, concat_axis=2, ti...  27.1 us
    psum x1, blocking collectives, on_device(): step_size = 1.0 / lax.psum(norm_part, 'qband')  25.1 us
    another operation x2, other arithmetic  24.9 us
  transfers between devices with their start and end apart: 1, of which 1 were waited for; matrix products, arithmetic and copies ran while one was open for 0% of the time, Pallas kernels for 0%

profile of v1, /device:TPU:1, one launch (start us, length us, event | category | flops | bytes accessed | tf_op | source)
XLA Modules:
  0.0 833.1 jit_solution(6439644070515327992)
XLA Ops:
  0.6 18.3 %multiply_convert_fusion = (bf16[1024,1024]{1,0:T(8,128)(2,1)S(1)}, bf16[1024,1024]{1,0:T(8,128)(2,1)S(1)}) fusion(), kind=kLoop, calls=%fused_computation.49 | loop fusion | flops 26214400 | bytes 4194304 | tf_op jit(solution)/shard_map/convert.3
  23.3 6.4 copy.9
  29.7 22.7 %convolution_bitcast_fusion = f32[2,1024,1,2048]{3,1,0,2:T(8,128)} fusion(bf16[1024,1024]{1,0:T(8,128)(2,1)} %copy-done.3, bf16[1024,1024]{1,0:T(8,128)(2,1)} %copy-done.4, bf16[2,1024,1024]{2,1,0:T(8,128)(2,1)} %bitcast.67, bf16[1,1024,1024]{2,1,0:T(8,128)(2,1)S(1)} %copy-done), kind=kOutput, calls=%fused_computation.32 | convolution fusion | flops 12895387648 | bytes 27262976 | tf_op jit(solution)/shard_map/ckty,yj->cktj/dot_general | solution.py:65
  52.4 6.6 fusion.30
  59.4 6.3 copy.10
  65.7 11.9 %all-to-all-start = ((bf16[2,1024,1,1024]{3,0,2,1:T(2,128)(2,1)}), bf16[2,1024,1,1024]{3,0,2,1:T(2,128)(2,1)}, u32[]{:S(2)}, u32[]{:S(2)}) async-start(bf16[2,1024,1,1024]{3,0,2,1:T(2,128)(2,1)} %copy.10), calls=%async_computation | async-start | bytes 8388608 | tf_op jit(solution)/shard_map/all_to_all | solution.py:70
  77.9 25.1 %psum.21 = f32[2]{0:T(128)S(1)} all-reduce(f32[2]{0:T(128)S(1)} %multiply_reduce_fusion), channel_id=1, replica_groups=mesh['tm'=32,'qband'=4] {'qband'}, use_global_device_ids=true, to_apply=%region_8.9 | all-reduce | flops 2 | bytes 16 | tf_op jit(solution)/shard_map/psum | solution.py:85
  103.1 27.1 %all-to-all-done = bf16[2,1024,1,1024]{3,0,2,1:T(2,128)(2,1)} async-done(((bf16[2,1024,1,1024]{3,0,2,1:T(2,128)(2,1)}), bf16[2,1024,1,1024]{3,0,2,1:T(2,128)(2,1)}, u32[]{:S(2)}, u32[]{:S(2)}) %all-to-all-start) | async-done | bytes 4194336 | tf_op jit(solution)/shard_map/all_to_all | solution.py:70
  139.1 267.7 %while.22 = (s32[]{:T(128)}, f32[16,8,1024]{2,1,0:T(8,128)S(1)}, s32[16]{0:T(128)S(1)}, bf16[2,8,256,1024]{3,2,1,0:T(8,128)(2,1)}, bf16[2,8,128,1024]{3,2,1,0:T(...) while((s32[]{:T(128)}, f32[16,8,1024]{2,1,0:T(8,128)S(1)}, s32[16]{0:T(128)S(1)}, ...), condition=%wide.region_2.3_spmd.clone, body=%wide.region_0.2_spmd.clone.sunk | while | flops 11534599 | bytes 25265328 | solution.py:45
  141.6 8.9 %convert_subtract_fusion.2 = f32[2,8,128,1024]{3,2,1,0:T(8,128)} fusion(bf16[2,8,128,1024]{3,2,1,0:T(8,128)(2,1)} %get-tuple-element.218, bf16[2,8,256,1024]{3,2,1,0:T(8,128)(2,1)} %get-tuple-element.217, s32[]{:T(128)S(6)} %select_n.30), kind=kLoop, calls=%fused_computation.2.clone.1 | loop fusion | flops 6291456 | bytes 16777220 | tf_op jit(solution)/shard_map/while/body/eval_jaxpr/sub | solution.py:39
  158.4 8.9 %convert_subtract_fusion.2 = f32[2,8,128,1024]{3,2,1,0:T(8,128)} fusion(bf16[2,8,128,1024]{3,2,1,0:T(8,128)(2,1)} %get-tuple-element.218, bf16[2,8,256,1024]{3,2,1,0:T(8,128)(2,1)} %get-tuple-element.217, s32[]{:T(128)S(6)} %select_n.30), kind=kLoop, calls=%fused_computation.2.clone.1 | loop fusion | flops 6291456 | bytes 16777220 | tf_op jit(solution)/shard_map/while/body/eval_jaxpr/sub | solution.py:39
  175.1 8.9 %convert_subtract_fusion.2 = f32[2,8,128,1024]{3,2,1,0:T(8,128)} fusion(bf16[2,8,128,1024]{3,2,1,0:T(8,128)(2,1)} %get-tuple-element.218, bf16[2,8,256,1024]{3,2,1,0:T(8,128)(2,1)} %get-tuple-element.217, s32[]{:T(128)S(6)} %select_n.30), kind=kLoop, calls=%fused_computation.2.clone.1 | loop fusion | flops 6291456 | bytes 16777220 | tf_op jit(solution)/shard_map/while/body/eval_jaxpr/sub | solution.py:39
  191.8 8.9 %convert_subtract_fusion.2 = f32[2,8,128,1024]{3,2,1,0:T(8,128)} fusion(bf16[2,8,128,1024]{3,2,1,0:T(8,128)(2,1)} %get-tuple-element.218, bf16[2,8,256,1024]{3,2,1,0:T(8,128)(2,1)} %get-tuple-element.217, s32[]{:T(128)S(6)} %select_n.30), kind=kLoop, calls=%fused_computation.2.clone.1 | loop fusion | flops 6291456 | bytes 16777220 | tf_op jit(solution)/shard_map/while/body/eval_jaxpr/sub | solution.py:39
  208.6 8.9 %convert_subtract_fusion.2 = f32[2,8,128,1024]{3,2,1,0:T(8,128)} fusion(bf16[2,8,128,1024]{3,2,1,0:T(8,128)(2,1)} %get-tuple-element.218, bf16[2,8,256,1024]{3,2,1,0:T(8,128)(2,1)} %get-tuple-element.217, s32[]{:T(128)S(6)} %select_n.30), kind=kLoop, calls=%fused_computation.2.clone.1 | loop fusion | flops 6291456 | bytes 16777220 | tf_op jit(solution)/shard_map/while/body/eval_jaxpr/sub | solution.py:39
  225.3 8.9 %convert_subtract_fusion.2 = f32[2,8,128,1024]{3,2,1,0:T(8,128)} fusion(bf16[2,8,128,1024]{3,2,1,0:T(8,128)(2,1)} %get-tuple-element.218, bf16[2,8,256,1024]{3,2,1,0:T(8,128)(2,1)} %get-tuple-element.217, s32[]{:T(128)S(6)} %select_n.30), kind=kLoop, calls=%fused_computation.2.clone.1 | loop fusion | flops 6291456 | bytes 16777220 | tf_op jit(solution)/shard_map/while/body/eval_jaxpr/sub | solution.py:39
  242.0 8.9 %convert_subtract_fusion.2 = f32[2,8,128,1024]{3,2,1,0:T(8,128)} fusion(bf16[2,8,128,1024]{3,2,1,0:T(8,128)(2,1)} %get-tuple-element.218, bf16[2,8,256,1024]{3,2,1,0:T(8,128)(2,1)} %get-tuple-element.217, s32[]{:T(128)S(6)} %select_n.30), kind=kLoop, calls=%fused_computation.2.clone.1 | loop fusion | flops 6291456 | bytes 16777220 | tf_op jit(solution)/shard_map/while/body/eval_jaxpr/sub | solution.py:39
  258.7 8.9 %convert_subtract_fusion.2 = f32[2,8,128,1024]{3,2,1,0:T(8,128)} fusion(bf16[2,8,128,1024]{3,2,1,0:T(8,128)(2,1)} %get-tuple-element.218, bf16[2,8,256,1024]{3,2,1,0:T(8,128)(2,1)} %get-tuple-element.217, s32[]{:T(128)S(6)} %select_n.30), kind=kLoop, calls=%fused_computation.2.clone.1 | loop fusion | flops 6291456 | bytes 16777220 | tf_op jit(solution)/shard_map/while/body/eval_jaxpr/sub | solution.py:39
  275.5 8.9 %convert_subtract_fusion.2 = f32[2,8,128,1024]{3,2,1,0:T(8,128)} fusion(bf16[2,8,128,1024]{3,2,1,0:T(8,128)(2,1)} %get-tuple-element.218, bf16[2,8,256,1024]{3,2,1,0:T(8,128)(2,1)} %get-tuple-element.217, s32[]{:T(128)S(6)} %select_n.30), kind=kLoop, calls=%fused_computation.2.clone.1 | loop fusion | flops 6291456 | bytes 16777220 | tf_op jit(solution)/shard_map/while/body/eval_jaxpr/sub | solution.py:39
  292.2 8.9 %convert_subtract_fusion.2 = f32[2,8,128,1024]{3,2,1,0:T(8,128)} fusion(bf16[2,8,128,1024]{3,2,1,0:T(8,128)(2,1)} %get-tuple-element.218, bf16[2,8,256,1024]{3,2,1,0:T(8,128)(2,1)} %get-tuple-element.217, s32[]{:T(128)S(6)} %select_n.30), kind=kLoop, calls=%fused_computation.2.clone.1 | loop fusion | flops 6291456 | bytes 16777220 | tf_op jit(solution)/shard_map/while/body/eval_jaxpr/sub | solution.py:39
  308.9 8.9 %convert_subtract_fusion.2 = f32[2,8,128,1024]{3,2,1,0:T(8,128)} fusion(bf16[2,8,128,1024]{3,2,1,0:T(8,128)(2,1)} %get-tuple-element.218, bf16[2,8,256,1024]{3,2,1,0:T(8,128)(2,1)} %get-tuple-element.217, s32[]{:T(128)S(6)} %select_n.30), kind=kLoop, calls=%fused_computation.2.clone.1 | loop fusion | flops 6291456 | bytes 16777220 | tf_op jit(solution)/shard_map/while/body/eval_jaxpr/sub | solution.py:39
  325.7 8.9 %convert_subtract_fusion.2 = f32[2,8,128,1024]{3,2,1,0:T(8,128)} fusion(bf16[2,8,128,1024]{3,2,1,0:T(8,128)(2,1)} %get-tuple-element.218, bf16[2,8,256,1024]{3,2,1,0:T(8,128)(2,1)} %get-tuple-element.217, s32[]{:T(128)S(6)} %select_n.30), kind=kLoop, calls=%fused_computation.2.clone.1 | loop fusion | flops 6291456 | bytes 16777220 | tf_op jit(solution)/shard_map/while/body/eval_jaxpr/sub | solution.py:39
  342.4 8.9 %convert_subtract_fusion.2 = f32[2,8,128,1024]{3,2,1,0:T(8,128)} fusion(bf16[2,8,128,1024]{3,2,1,0:T(8,128)(2,1)} %get-tuple-element.218, bf16[2,8,256,1024]{3,2,1,0:T(8,128)(2,1)} %get-tuple-element.217, s32[]{:T(128)S(6)} %select_n.30), kind=kLoop, calls=%fused_computation.2.clone.1 | loop fusion | flops 6291456 | bytes 16777220 | tf_op jit(solution)/shard_map/while/body/eval_jaxpr/sub | solution.py:39
  359.1 8.9 %convert_subtract_fusion.2 = f32[2,8,128,1024]{3,2,1,0:T(8,128)} fusion(bf16[2,8,128,1024]{3,2,1,0:T(8,128)(2,1)} %get-tuple-element.218, bf16[2,8,256,1024]{3,2,1,0:T(8,128)(2,1)} %get-tuple-element.217, s32[]{:T(128)S(6)} %select_n.30), kind=kLoop, calls=%fused_computation.2.clone.1 | loop fusion | flops 6291456 | bytes 16777220 | tf_op jit(solution)/shard_map/while/body/eval_jaxpr/sub | solution.py:39
  375.9 8.9 %convert_subtract_fusion.2 = f32[2,8,128,1024]{3,2,1,0:T(8,128)} fusion(bf16[2,8,128,1024]{3,2,1,0:T(8,128)(2,1)} %get-tuple-element.218, bf16[2,8,256,1024]{3,2,1,0:T(8,128)(2,1)} %get-tuple-element.217, s32[]{:T(128)S(6)} %select_n.30), kind=kLoop, calls=%fused_computation.2.clone.1 | loop fusion | flops 6291456 | bytes 16777220 | tf_op jit(solution)/shard_map/while/body/eval_jaxpr/sub | solution.py:39
  392.6 8.9 %convert_subtract_fusion.2 = f32[2,8,128,1024]{3,2,1,0:T(8,128)} fusion(bf16[2,8,128,1024]{3,2,1,0:T(8,128)(2,1)} %get-tuple-element.218, bf16[2,8,256,1024]{3,2,1,0:T(8,128)(2,1)} %get-tuple-element.217, s32[]{:T(128)S(6)} %select_n.30), kind=kLoop, calls=%fused_computation.2.clone.1 | loop fusion | flops 6291456 | bytes 16777220 | tf_op jit(solution)/shard_map/while/body/eval_jaxpr/sub | solution.py:39
  407.2 64.3 %all-reduce.1 = (f32[64,16]{1,0:T(8,128)S(1)}, f32[64]{0:T(128)S(1)}) all-reduce(f32[64,16]{1,0:T(8,128)S(1)} %fusion.44, f32[64]{0:T(128)S(1)} %convert_reduce_fusion), channel_id=1, replica_groups=mesh['tm'=32,'qband'=4] {'tm','qband'}, use_global_device_ids=true, to_apply=%region_4.5 | all-reduce | flops 1088 | bytes 8704 | tf_op jit(solution)/shard_map/psum | solution.py:79
  471.6 360.9 %while.23 = (s32[]{:T(128)}, f32[2,256]{1,0:T(2,128)S(1)}, f32[2]{0:T(128)S(1)}, f32[2,16]{1,0:T(2,128)S(1)}, f32[16]{0:T(128)S(1)}, /*index=5*/f32[2,256]{1,0:T(2,128)S(1)}, s32[]{:T(128)}, s32[]{:T(128)}, f32[]{:T(128)}) while((s32[]{:T(128)}, f32[2,256]{1,0:T(2,128)S(1)}, f32[2]{0:T(128)S(1)}, f32[2,16]{1,0:T(2,128)S(1)}, ...), condition=%wide.region_11.12_spmd.clone, body=%wide.region_9.11_spmd.clone.sunk | while | flops 248451 | bytes 20596 | solution.py:93
  471.9 5.5 all-gather.4
  478.0 5.1 all-gather.4
  483.6 5.1 all-gather.4
  489.2 5.1 all-gather.4
  494.9 5.1 all-gather.4
  500.5 5.1 all-gather.4
  506.1 5.1 all-gather.4
  511.8 5.1 all-gather.4
  517.4 5.1 all-gather.4
  523.0 5.1 all-gather.4
  528.7 5.1 all-gather.4
  534.3 5.1 all-gather.4
  539.9 5.1 all-gather.4
  545.5 5.1 all-gather.4
  551.2 5.1 all-gather.4
  556.8 5.1 all-gather.4
  562.4 5.1 all-gather.4
  568.1 5.1 all-gather.4
  573.7 5.1 all-gather.4
  579.3 5.1 all-gather.4
  585.0 5.1 all-gather.4
  (527 shorter events, 352.2 us)
Async XLA Ops:
  0.6 29.1 %copy-start = (bf16[1,1024,1024]{2,1,0:T(8,128)(2,1)S(1)}, bf16[1,1024,1024]{2,1,0:T(8,128)(2,1)}, u32[]{:S(2)}) copy-start(bf16[1,1024,1024]{2,1,0:T(8,128)(2,1)} %param.8) | copy-start | bytes 6291460
  19.0 1.3 copy-start.3
  19.0 2.0 copy-start.4
  65.7 12.0 %copy-start.7 = (f32[2,256]{1,0:T(2,128)S(1)}, f32[2,256]{1,0:T(2,128)}, u32[]{:S(2)}) copy-start(f32[2,256]{1,0:T(2,128)} %param.11) | copy-start | bytes 6148
  65.7 12.0 %copy-start.8 = (s32[16]{0:T(128)S(1)}, s32[16]{0:T(128)}, u32[]{:S(2)}) copy-start(s32[16]{0:T(128)} %param.9) | copy-start | bytes 196
  65.7 37.3 %copy-start.9 = (s32[8,1]{0,1:T(1,128)S(1)}, s32[8,1]{0,1:T(1,128)}, u32[]{:S(2)}) copy-start(s32[8,1]{0,1:T(1,128)} %param.10) | copy-start | bytes 100
  65.7 64.4 %all-to-all-start = ((bf16[2,1024,1,1024]{3,0,2,1:T(2,128)(2,1)}), bf16[2,1024,1,1024]{3,0,2,1:T(2,128)(2,1)}, u32[]{:S(2)}, u32[]{:S(2)}) async-start(bf16[2,1024,1,1024]{3,0,2,1:T(2,128)(2,1)} %copy.10), calls=%async_computation | async-start | bytes 8388608 | tf_op jit(solution)/shard_map/all_to_all | solution.py:70
  134.6 4.5 copy-start.2
  406.8 425.7 %copy-start.5 = (f32[16,8,1024]{2,1,0:T(8,128)}, f32[16,8,1024]{2,1,0:T(8,128)S(1)}, u32[]{:S(2)}) copy-start(f32[16,8,1024]{2,1,0:T(8,128)S(1)} %get-tuple-element.59) | copy-start | bytes 1572868
  406.8 426.3 %copy-start.1 = (bf16[1,1024,1024]{2,1,0:T(8,128)(2,1)S(1)}, bf16[1,1024,1024]{2,1,0:T(8,128)(2,1)}, u32[]{:S(2)}) copy-start(bf16[1,1024,1024]{2,1,0:T(8,128)(2,1)} %param.8) | copy-start | bytes 6291460
  832.5 0.6 copy-start.6
